TPU v7x, 512 devices: a whole 4x8x8 slice. The times are simulated.
512 devices in a mesh: grp: 16 (over x, z_lo), ep: 32 (over y, z_hi, core).
Axes of the slice: x: 4, y: 8, z: 8 (z_hi: 2, z_lo: 4; z = z_hi * 4 + z_lo), core: 2. Of those that a mesh axis runs over, the one named last changes fastest.
Arguments:
- slot_hidden: bfloat16 [65536, 8, 768], P(('grp', 'ep')), may hold values from -6 to 6
- expert_ids: int32 [65536, 8], P(('grp', 'ep')), may hold values from 0 to 63, all different within a row; in each aligned block of 128 rows (0 to 127, 128 to 255, ...) at most 24 rows name the same one
- gate_fixed: int32 [65536, 8], P(('grp', 'ep')), may hold values from 1 to 65535
- master: float32 [64, 768, 2048], P('ep', 'grp'), may hold values from -6 to 6
- moment_one: bfloat16 [64, 768, 2048], P('ep', 'grp'), may hold values from -3 to 3
- moment_two: bfloat16 [64, 768, 2048], P('ep', 'grp'), may hold values from 0.0099487305 to 2
- gradient: bfloat16 [64, 768, 2048], P('ep', 'grp'), may hold values from -6 to 6
Outputs:
- mixed: bfloat16 [65536, 2048], P(('grp', 'ep'))
- backup: float32 [64, 768, 2048], P('ep', 'grp')
Inputs may be any that keep to these rules, and one draw needn't show every extreme that they name: `expert_ids`: in each aligned block of 128 rows (the rows of one device) no expert is named by more than 24 rows, a bound that some block reaches; the 8 experts of a row differ.
All inputs are finite; a program needn't handle non-finite values.
Results may differ from a plain program's by a relative error of at most 0.0057.
Values may be sent and summed in bfloat16 or wider, within the bound.
No kernel may reach another device: no remote copies, remote signals or barrier semaphores. Data moves between devices by JAX's collectives and lax.ppermute only.
A program may use at most 64 MiB of HBM per device.

v0:
```python
import math
import jax
import jax.numpy as jnp
from jax import lax
from jax.sharding import PartitionSpec as P

beta_one = 0.9
beta_two = 0.95
corr_one = 1.0 - 0.9**40
corr_two = 1.0 - 0.95**40
learn_rate = 0.05
decay_rate = 0.1
adam_eps = 1e-08
gate_unit = 65536.0


def adamw_step(master, moment_one, moment_two, gradient):
    widened = gradient.astype(jnp.float32)
    first_moment = beta_one * moment_one.astype(jnp.float32) + (1.0 - beta_one) * widened
    second_moment = beta_two * moment_two.astype(jnp.float32) + (1.0 - beta_two) * widened * widened
    return (
        first_moment / corr_one / (jnp.sqrt(second_moment / corr_two) + adam_eps)
        + decay_rate * master
    )


def slot_positions(ids, capacity):
    count = ids.shape[0]
    rows = lax.broadcasted_iota(jnp.int32, (count, count), 0)
    cols = lax.broadcasted_iota(jnp.int32, (count, count), 1)
    same = (ids[:, None] == ids[None, :]) & (cols < rows)
    slot_index = jnp.sum(same.astype(jnp.int32), axis=1)
    return ids * capacity + slot_index


def body(slot_hidden, expert_ids, gate_fixed, master, moment_one, moment_two, gradient):
    groups = lax.axis_size("grp")
    ranks = lax.axis_size("ep")
    local_experts = master.shape[0]
    experts = local_experts * ranks
    tok_count, top_count, hidden_width = slot_hidden.shape
    width = master.shape[2]
    capacity = max(2, tok_count * top_count // experts + tok_count * top_count // (2 * experts))
    slots = experts * capacity
    scaling = 1.0 / math.sqrt(hidden_width)
    step_dir = adamw_step(master, moment_one, moment_two, gradient)
    updated = master - learn_rate * step_dir
    weights = updated.astype(jnp.bfloat16)
    gathered = lax.all_gather(weights, "grp", axis=1, tiled=True)
    shift = groups // 2
    backup = lax.ppermute(step_dir, "grp", [(s, (s + shift) % groups) for s in range(groups)])
    pairs = tok_count * top_count
    positions = slot_positions(expert_ids.reshape(pairs), capacity)
    slot_ids = lax.broadcasted_iota(jnp.int32, (slots, pairs), 0)
    placing = (positions[None, :] == slot_ids).astype(jnp.bfloat16)
    outgoing = jnp.dot(
        placing, slot_hidden.reshape(pairs, hidden_width), preferred_element_type=jnp.float32
    ).astype(jnp.bfloat16)
    outgoing = outgoing.reshape(experts, capacity, hidden_width)
    arrived = lax.all_to_all(outgoing, "ep", split_axis=0, concat_axis=1, tiled=True)
    product = jnp.einsum("erh,ehd->erd", arrived, gathered, preferred_element_type=jnp.float32)
    results = (product * scaling).astype(jnp.bfloat16)
    tiles = results.reshape(local_experts, ranks, capacity, width).transpose(1, 0, 2, 3)
    returned = lax.all_to_all(tiles, "ep", split_axis=0, concat_axis=0, tiled=True)
    returned = returned.reshape(slots, width)
    factors = gate_fixed.astype(jnp.float32) / gate_unit
    token_pos = positions.reshape(tok_count, top_count)
    slot_row = lax.broadcasted_iota(jnp.int32, (tok_count, top_count, slots), 2)
    combine = jnp.sum(
        jnp.where(token_pos[:, :, None] == slot_row, factors[:, :, None], 0.0), axis=1
    )
    combine_hi = combine.astype(jnp.bfloat16)
    combine_lo = (combine - combine_hi.astype(jnp.float32)).astype(jnp.bfloat16)
    mixed = jnp.dot(combine_hi, returned, preferred_element_type=jnp.float32) + jnp.dot(
        combine_lo, returned, preferred_element_type=jnp.float32
    )
    return (mixed.astype(jnp.bfloat16), backup)


def solution(mesh):
    tokens = P(("grp", "ep"), None, None)
    pair_spec = P(("grp", "ep"), None)
    state = P("ep", "grp", None)
    in_specs = (tokens, pair_spec, pair_spec, state, state, state, state)
    out_specs = (pair_spec, state)
    return jax.shard_map(body, mesh=mesh, in_specs=in_specs, out_specs=out_specs, check_vma=False)
```

profile of v0, /device:TPU:21, one launch (start us, length us, event | category | flops | bytes accessed | tf_op | source)
XLA Modules:
  0.0 426.3 jit_solution(7426811078113007954)
XLA Ops:
  7.2 0.0 copy-start
  7.2 0.0 all-gather.2.cloned.1.call-start
  7.2 3.3 subtract_convert_fusion.1
  10.5 0.0 all-gather.2.cloned.1.call-update
  10.5 0.8 copy.24
  11.3 0.1 eq.31
  11.4 0.5 convert_reduce_fusion
  11.9 0.0 copy-done
  11.9 3.0 fusion.2
  15.0 75.1 %all_to_all.23 = bf16[64,24,768]{2,1,0:T(8,128)(2,1)S(1)} all-to-all(bf16[64,24,768]{2,1,0:T(8,128)(2,1)S(1)} %bitcast.21), channel_id=1, replica_groups=mesh['grp'=16,'ep'=32] {'ep'}, dimensions={0} | all-to-all | bytes 4718592 | tf_op jit(solution)/shard_map/all_to_all | solution.py:60
  90.1 1.6 copy.28
  91.6 118.8 %all-gather.2.cloned.1.call-done = bf16[2,768,2048]{2,1,0:T(8,128)(2,1)} async-done(((bf16[2,48,2048]{2,1,0:T(8,128)(2,1)}), bf16[2,768,2048]{2,1,0:T(8,128)(2,1)}) %all-gather.2.cloned.1.call-update) | async-done | bytes 6291472 | tf_op jit(solution)/shard_map/all_gather | solution.py:49
  210.5 7.9 %multiply_convert_fusion = bf16[2,768,2048]{2,1,0:T(8,128)(2,1)S(1)} fusion(bf16[2,768,768]{2,1,0:T(8,128)(2,1)} %bitcast.20, bf16[2,768,2048]{2,1,0:T(8,128)(2,1)} %all-gather.2.cloned.1.call-done), kind=kOutput, calls=%fused_computation | convolution fusion | flops 4838129664 | bytes 14942208 | tf_op jit(solution)/shard_map/erh,ehd->erd/dot_general | solution.py:61
  218.3 3.2 copy.31
  221.6 0.0 copy-start.1
  221.6 0.0 copy-start.2
  221.6 11.1 %all-to-all-start.1 = ((bf16[32,2,24,2048]{3,2,1,0:T(8,128)(2,1)}), bf16[32,2,24,2048]{3,2,1,0:T(8,128)(2,1)}, u32[]{:S(2)}, u32[]{:S(2)}) async-start(bf16[32,2,24,2048]{3,2,1,0:T(8,128)(2,1)} %bitcast.17), calls=%async_computation.1 | async-start | bytes 12582912 | tf_op jit(solution)/shard_map/all_to_all | solution.py:64
  232.7 4.1 collective-permute-start
  236.7 0.1 reduce_sum.21
  236.9 0.0 copy-done.1
  236.9 0.1 copy.26
  237.0 0.0 copy-done.2
  237.0 0.1 copy.27
  237.1 2.0 select_reduce_fusion
  239.2 16.0 %collective-permute-done = f32[2,48,2048]{2,1,0:T(8,128)S(1)} collective-permute-done((f32[2,48,2048]{2,1,0:T(8,128)}, f32[2,48,2048]{2,1,0:T(8,128)S(1)}, u32[]{:S(2)}, u32[]{:S(2)}) %collective-permute-start) | collective-permute-done | bytes 786464 | tf_op jit(solution)/shard_map/ppermute | solution.py:51
  255.1 155.0 %all-to-all-done.1 = bf16[32,2,24,2048]{3,2,1,0:T(8,128)(2,1)} async-done(((bf16[32,2,24,2048]{3,2,1,0:T(8,128)(2,1)}), bf16[32,2,24,2048]{3,2,1,0:T(8,128)(2,1)}, u32[]{:S(2)}, u32[]{:S(2)}) %all-to-all-start.1) | async-done | bytes 6291488 | tf_op jit(solution)/shard_map/all_to_all | solution.py:64
  410.1 3.8 fusion.15
  413.9 4.7 %fusion.4 = bf16[128,2048]{1,0:T(8,128)(2,1)} fusion(f32[128,2048]{1,0:T(8,128)S(1)} %fusion.15, bf16[1536,2048]{1,0:T(8,128)(2,1)} %bitcast.7, f32[128,1536]{1,0:T(8,128)S(1)} %select_reduce_fusion), kind=kOutput, calls=%fused_computation.12 | convolution fusion | flops 806617088 | bytes 8650752 | tf_op jit(solution)/shard_map/dot_general | solution.py:74
  418.6 0.9 copy.33
  (4 shorter events, 0.1 us)
Async XLA Ops:
  7.2 4.8 %copy-start = (bf16[128,8,768]{2,1,0:T(8,128)(2,1)S(1)}, bf16[128,8,768]{2,1,0:T(8,128)(2,1)}, u32[]{:S(2)}) copy-start(bf16[128,8,768]{2,1,0:T(8,128)(2,1)} %param.7) | copy-start | bytes 4718596
  7.2 203.3 %all-gather.2.cloned.1.call-start = ((), (), s32[]{:S(2)}) async-start(), calls=%async_computation.2 | async-start | bytes 6684672 | tf_op jit(solution)/shard_map/all_gather | solution.py:49
  221.6 15.3 %copy-start.1 = (s32[128,8]{0,1:T(8,128)S(1)}, s32[128,8]{0,1:T(8,128)}, u32[]{:S(2)}) copy-start(s32[128,8]{0,1:T(8,128)} %param.8) | copy-start | bytes 12292
  221.6 15.4 %copy-start.2 = (s32[128,8]{0,1:T(8,128)S(1)}, s32[128,8]{0,1:T(8,128)}, u32[]{:S(2)}) copy-start(s32[128,8]{0,1:T(8,128)} %param.9) | copy-start | bytes 12292
  221.6 188.5 %all-to-all-start.1 = ((bf16[32,2,24,2048]{3,2,1,0:T(8,128)(2,1)}), bf16[32,2,24,2048]{3,2,1,0:T(8,128)(2,1)}, u32[]{:S(2)}, u32[]{:S(2)}) async-start(bf16[32,2,24,2048]{3,2,1,0:T(8,128)(2,1)} %bitcast.17), calls=%async_computation.1 | async-start | bytes 12582912 | tf_op jit(solution)/shard_map/all_to_all | solution.py:64
  232.7 22.5 %collective-permute-start = (f32[2,48,2048]{2,1,0:T(8,128)}, f32[2,48,2048]{2,1,0:T(8,128)S(1)}, u32[]{:S(2)}, u32[]{:S(2)}) collective-permute-start(f32[2,48,2048]{2,1,0:T(8,128)} %get-tuple-element.3), channel_id=1, source_target_pairs={{0,256},{32,288},{64,320},{96,352},{128,384},{160,416},{192,448},{... | collective-permute-start | bytes 2359304 | tf_op jit(solution)/shard_map/ppermute | solution.py:51
Sparse Core Ops, SparseCore 0:
  10.7 199.7 all-gather.1
where the time goes:
time: 427 us; the launch traced here: 426 us
  waiting for transfers between devices  290 us (68%)
  blocking collectives  75.1 us (18%)
  matrix products  19.3 us (5%)
  starting transfers between devices  15.2 us (4%)
  between operations  14.1 us (3%)
  local copies, waits for them, and re-layouts  6.93 us (2%)
  other arithmetic  5.84 us (1%)
    all_to_all x1, waiting for transfers between devices, body(): lax.all_to_all(tiles, 'ep', split_axis=0, concat_axis=0, tiled=True)  155 us
    all_gather x1, waiting for transfers between devices, body(): gathered = lax.all_gather(weights, 'grp', axis=1, tiled=True)  119 us
    all_to_all x1, blocking collectives, body(): lax.all_to_all(outgoing, 'ep', split_axis=0, concat_axis=1, tiled=True)  75.1 us
    ppermute x1, waiting for transfers between devices, body(): lax.ppermute(step_dir, 'grp', [(s, (s + shift) % groups) for s in range(g...  16 us
    all_to_all x1, starting transfers between devices, body(): lax.all_to_all(tiles, 'ep', split_axis=0, concat_axis=0, tiled=True)  11.1 us
  transfers between devices with their start and end apart: 3, of which 3 were waited for; matrix products, arithmetic and copies ran while one was open for 2% of the time, Pallas kernels for 0%

commit v1 on v0

--- a/solution.py
+++ b/solution.py
@@ -57,7 +57,12 @@
         placing, slot_hidden.reshape(pairs, hidden_width), preferred_element_type=jnp.float32
     ).astype(jnp.bfloat16)
     outgoing = outgoing.reshape(experts, capacity, hidden_width)
-    arrived = lax.all_to_all(outgoing, "ep", split_axis=0, concat_axis=1, tiled=True)
+    arrived = jnp.concatenate(
+        lax.all_to_all(
+            jnp.stack(jnp.split(outgoing, lax.psum(1, "ep"), axis=0), axis=0), "ep", 0, 0
+        ),
+        axis=1,
+    )
     product = jnp.einsum("erh,ehd->erd", arrived, gathered, preferred_element_type=jnp.float32)
     results = (product * scaling).astype(jnp.bfloat16)
     tiles = results.reshape(local_experts, ranks, capacity, width).transpose(1, 0, 2, 3)

time: 427 us -> 425 us (level)
  no operation moved by 1% of the time
where the time goes in v1:
time: 425 us
  waiting for transfers between devices  289 us (68%)
  blocking collectives  75.1 us (18%)
  matrix products  19.3 us (5%)
  starting transfers between devices  15.2 us (4%)
  between operations  14.4 us (3%)
  local copies, waits for them, and re-layouts  6.66 us (2%)
  other arithmetic  5.84 us (1%)
    all_to_all x1, waiting for transfers between devices, body(): lax.all_to_all(tiles, 'ep', split_axis=0, concat_axis=0, tiled=True)  154 us
    all_gather x1, waiting for transfers between devices, body(): gathered = lax.all_gather(weights, 'grp', axis=1, tiled=True)  119 us
    all_to_all x1, blocking collectives, body(): lax.all_to_all(jnp.stack(jnp.split(outgoing, lax.psum(1, 'ep'), axis=0),...  75.1 us
    ppermute x1, waiting for transfers between devices, body(): lax.ppermute(step_dir, 'grp', [(s, (s + shift) % groups) for s in range(g...  16 us
    all_to_all x1, starting transfers between devices, body(): lax.all_to_all(tiles, 'ep', split_axis=0, concat_axis=0, tiled=True)  11.1 us
  transfers between devices with their start and end apart: 3, of which 3 were waited for; matrix products, arithmetic and copies ran while one was open for 2% of the time, Pallas kernels for 0%

profile of v1, /device:TPU:21, one launch (start us, length us, event | category | flops | bytes accessed | tf_op | source)
XLA Modules:
  0.0 425.1 jit_solution(8661065646550280738)
XLA Ops:
  7.2 0.0 copy-start
  7.2 0.0 copy-start.1
  7.2 0.0 all-gather.2.cloned.1.call-start
  7.2 3.3 subtract_convert_fusion.1
  10.5 0.0 all-gather.2.cloned.1.call-update
  10.5 0.0 copy-done.1
  10.5 0.1 copy.24
  10.6 0.1 eq.31
  10.7 0.5 convert_reduce_fusion
  11.3 0.0 copy-done
  11.3 3.0 fusion.2
  14.3 0.1 fusion.19
  14.6 0.1 fusion.18
  15.0 75.1 %all_to_all.10 = bf16[32,2,24,768]{3,2,1,0:T(8,128)(2,1)S(1)} all-to-all(bf16[32,2,24,768]{3,2,1,0:T(8,128)(2,1)S(1)} %constant_dynamic-update-slice_fusion), channel_id=1, replica_groups=mesh['grp'=16,'ep'=32] {'ep'}, dimensions={0} | all-to-all | bytes 4718592 | tf_op jit(solution)/shard_map/all_to_all | solution.py:61
  90.1 1.6 copy.28
  91.7 118.8 %all-gather.2.cloned.1.call-done = bf16[2,768,2048]{2,1,0:T(8,128)(2,1)} async-done(((bf16[2,48,2048]{2,1,0:T(8,128)(2,1)}), bf16[2,768,2048]{2,1,0:T(8,128)(2,1)}) %all-gather.2.cloned.1.call-update) | async-done | bytes 6291472 | tf_op jit(solution)/shard_map/all_gather | solution.py:49
  210.5 7.8 %multiply_convert_fusion = bf16[2,768,2048]{2,1,0:T(8,128)(2,1)S(1)} fusion(bf16[2,768,768]{2,1,0:T(8,128)(2,1)} %bitcast.49, bf16[2,768,2048]{2,1,0:T(8,128)(2,1)} %all-gather.2.cloned.1.call-done), kind=kOutput, calls=%fused_computation | convolution fusion | flops 4838129664 | bytes 14942208 | tf_op jit(solution)/shard_map/erh,ehd->erd/dot_general | solution.py:66
  218.4 3.2 copy.31
  221.6 0.0 copy-start.2
  221.6 11.1 %all-to-all-start.1 = ((bf16[32,2,24,2048]{3,2,1,0:T(8,128)(2,1)}), bf16[32,2,24,2048]{3,2,1,0:T(8,128)(2,1)}, u32[]{:S(2)}, u32[]{:S(2)}) async-start(bf16[32,2,24,2048]{3,2,1,0:T(8,128)(2,1)} %bitcast.46), calls=%async_computation.1 | async-start | bytes 12582912 | tf_op jit(solution)/shard_map/all_to_all | solution.py:69
  232.7 4.1 collective-permute-start
  236.7 0.1 reduce_sum.21
  236.9 0.1 copy.26
  237.0 0.0 copy-done.2
  237.0 0.1 copy.27
  237.1 2.0 select_reduce_fusion
  239.2 16.0 %collective-permute-done = f32[2,48,2048]{2,1,0:T(8,128)S(1)} collective-permute-done((f32[2,48,2048]{2,1,0:T(8,128)}, f32[2,48,2048]{2,1,0:T(8,128)S(1)}, u32[]{:S(2)}, u32[]{:S(2)}) %collective-permute-start) | collective-permute-done | bytes 786464 | tf_op jit(solution)/shard_map/ppermute | solution.py:51
  255.1 153.8 %all-to-all-done.1 = bf16[32,2,24,2048]{3,2,1,0:T(8,128)(2,1)} async-done(((bf16[32,2,24,2048]{3,2,1,0:T(8,128)(2,1)}), bf16[32,2,24,2048]{3,2,1,0:T(8,128)(2,1)}, u32[]{:S(2)}, u32[]{:S(2)}) %all-to-all-start.1) | async-done | bytes 6291488 | tf_op jit(solution)/shard_map/all_to_all | solution.py:69
  408.9 3.8 fusion.15
  412.7 4.7 %fusion.4 = bf16[128,2048]{1,0:T(8,128)(2,1)} fusion(f32[128,2048]{1,0:T(8,128)S(1)} %fusion.15, bf16[1536,2048]{1,0:T(8,128)(2,1)} %bitcast.37, f32[128,1536]{1,0:T(8,128)S(1)} %select_reduce_fusion), kind=kOutput, calls=%fused_computation.12 | convolution fusion | flops 806617088 | bytes 8650752 | tf_op jit(solution)/shard_map/dot_general | solution.py:79
  417.4 0.9 copy.64
  (36 shorter events, 0.3 us)
Async XLA Ops:
  7.2 4.1 copy-start
  7.2 3.3 copy-start.1
  7.2 203.3 %all-gather.2.cloned.1.call-start = ((), (), s32[]{:S(2)}) async-start(), calls=%async_computation.2 | async-start | bytes 6684672 | tf_op jit(solution)/shard_map/all_gather | solution.py:49
  221.6 15.4 %copy-start.2 = (s32[128,8]{0,1:T(8,128)S(1)}, s32[128,8]{0,1:T(8,128)}, u32[]{:S(2)}) copy-start(s32[128,8]{0,1:T(8,128)} %param.9) | copy-start | bytes 12292
  221.6 187.3 %all-to-all-start.1 = ((bf16[32,2,24,2048]{3,2,1,0:T(8,128)(2,1)}), bf16[32,2,24,2048]{3,2,1,0:T(8,128)(2,1)}, u32[]{:S(2)}, u32[]{:S(2)}) async-start(bf16[32,2,24,2048]{3,2,1,0:T(8,128)(2,1)} %bitcast.46), calls=%async_computation.1 | async-start | bytes 12582912 | tf_op jit(solution)/shard_map/all_to_all | solution.py:69
  232.7 22.5 %collective-permute-start = (f32[2,48,2048]{2,1,0:T(8,128)}, f32[2,48,2048]{2,1,0:T(8,128)S(1)}, u32[]{:S(2)}, u32[]{:S(2)}) collective-permute-start(f32[2,48,2048]{2,1,0:T(8,128)} %get-tuple-element.3), channel_id=1, source_target_pairs={{0,256},{32,288},{64,320},{96,352},{128,384},{160,416},{192,448},{... | collective-permute-start | bytes 2359304 | tf_op jit(solution)/shard_map/ppermute | solution.py:51
Sparse Core Ops, SparseCore 0:
  10.7 199.7 all-gather.1

commit v2 on v0

--- a/solution.py
+++ b/solution.py
@@ -46,7 +46,10 @@
     step_dir = adamw_step(master, moment_one, moment_two, gradient)
     updated = master - learn_rate * step_dir
     weights = updated.astype(jnp.bfloat16)
-    gathered = lax.all_gather(weights, "grp", axis=1, tiled=True)
+    size = lax.axis_size("grp")
+    blocks = jnp.stack([weights for _ in range(size)])
+    blocks = lax.all_to_all(blocks, "grp", split_axis=0, concat_axis=0)
+    gathered = jnp.concatenate(blocks, axis=1)
     shift = groups // 2
     backup = lax.ppermute(step_dir, "grp", [(s, (s + shift) % groups) for s in range(groups)])
     pairs = tok_count * top_count

time: 427 us -> 442 us (1.035)
  the two profiles are of different devices: /device:TPU:21 before, /device:TPU:34 now
where the time goes in v2:
time: 442 us; the launch traced here: 441 us
  waiting for transfers between devices  357 us (81%)
  starting transfers between devices  44.4 us (10%)
  matrix products  17.7 us (4%)
  local copies, waits for them, and re-layouts  15.6 us (4%)
  other arithmetic  5.13 us (1%)
    all_to_all x1, waiting for transfers between devices, body(): lax.all_to_all(tiles, 'ep', split_axis=0, concat_axis=0, tiled=True)  150 us
    all_to_all x1, waiting for transfers between devices, body(): blocks = lax.all_to_all(blocks, 'grp', split_axis=0, concat_axis=0)  132 us
    all_to_all x1, waiting for transfers between devices, body(): lax.all_to_all(outgoing, 'ep', split_axis=0, concat_axis=1, tiled=True)  58.3 us
    all_to_all x1, starting transfers between devices, body(): lax.all_to_all(tiles, 'ep', split_axis=0, concat_axis=0, tiled=True)  18 us
    ppermute x1, waiting for transfers between devices, body(): lax.ppermute(step_dir, 'grp', [(s, (s + shift) % groups) for s in range(g...  17.4 us
    all_to_all x1, starting transfers between devices, body(): lax.all_to_all(outgoing, 'ep', split_axis=0, concat_axis=1, tiled=True)  15.9 us
  transfers between devices with their start and end apart: 4, of which 4 were waited for; matrix products, arithmetic and copies ran while one was open for 2% of the time, Pallas kernels for 0%

profile of v2, /device:TPU:34, one launch (start us, length us, event | category | flops | bytes accessed | tf_op | source)
XLA Modules:
  0.0 441.2 jit_solution(8775398326669913367)
XLA Ops:
  0.6 0.0 copy-start
  0.6 0.9 copy.32
  1.6 0.1 eq.31
  1.6 0.5 convert_reduce_fusion
  2.2 0.0 copy-done
  2.2 0.0 copy-start.2
  2.2 0.0 copy-start.3
  2.2 0.0 copy-start.4
  2.2 4.0 fusion.2
  6.3 15.9 %all-to-all-start = ((bf16[64,24,768]{2,1,0:T(8,128)(2,1)}), bf16[64,24,768]{2,1,0:T(8,128)(2,1)}, u32[]{:S(2)}, u32[]{:S(2)}) async-start(bf16[64,24,768]{2,1,0:T(8,128)(2,1)} %bitcast.22), calls=%async_computation | async-start | bytes 4718592 | tf_op jit(solution)/shard_map/all_to_all | solution.py:63
  22.1 0.0 copy-done.2
  22.2 0.0 copy-done.3
  22.2 0.0 copy-done.4
  22.2 2.6 subtract_convert_fusion.1
  24.7 58.3 %all-to-all-done = bf16[64,24,768]{2,1,0:T(8,128)(2,1)} async-done(((bf16[64,24,768]{2,1,0:T(8,128)(2,1)}), bf16[64,24,768]{2,1,0:T(8,128)(2,1)}, u32[]{:S(2)}, u32[]{:S(2)}) %all-to-all-start) | async-done | bytes 2359328 | tf_op jit(solution)/shard_map/all_to_all | solution.py:63
  83.0 3.4 stack.2
  86.5 7.2 %all-to-all-start.1 = ((bf16[16,2,48,2048]{3,2,1,0:T(8,128)(2,1)}), bf16[16,2,48,2048]{3,2,1,0:T(8,128)(2,1)}, u32[]{:S(2)}, u32[]{:S(2)}) async-start(bf16[16,2,48,2048]{3,2,1,0:T(8,128)(2,1)} %stack.2), calls=%async_computation.1 | async-start | bytes 12582912 | tf_op jit(solution)/shard_map/all_to_all | solution.py:51
  93.7 3.2 copy.36
  96.9 132.0 %all-to-all-done.1 = bf16[16,2,48,2048]{3,2,1,0:T(8,128)(2,1)} async-done(((bf16[16,2,48,2048]{3,2,1,0:T(8,128)(2,1)}), bf16[16,2,48,2048]{3,2,1,0:T(8,128)(2,1)}, u32[]{:S(2)}, u32[]{:S(2)}) %all-to-all-start.1) | async-done | bytes 6291488 | tf_op jit(solution)/shard_map/all_to_all | solution.py:51
  228.9 0.0 copy-start.1
  228.9 3.5 copy.37
  232.4 0.0 copy-done.1
  232.4 5.3 %multiply_convert_fusion = bf16[2,768,2048]{2,1,0:T(8,128)(2,1)S(1)} fusion(bf16[2,768,768]{2,1,0:T(8,128)(2,1)S(1)} %bitcast.23, bf16[2,768,2048]{2,1,0:T(8,128)(2,1)S(1)} %bitcast.20), kind=kOutput, calls=%fused_computation | convolution fusion | flops 4838129664 | bytes 14942208 | tf_op jit(solution)/shard_map/erh,ehd->erd/dot_general | solution.py:64
  237.6 3.2 copy.40
  240.9 0.0 copy-start.5
  240.9 0.0 copy-start.6
  240.9 18.0 %all-to-all-start.2 = ((bf16[32,2,24,2048]{3,2,1,0:T(8,128)(2,1)}), bf16[32,2,24,2048]{3,2,1,0:T(8,128)(2,1)}, u32[]{:S(2)}, u32[]{:S(2)}) async-start(bf16[32,2,24,2048]{3,2,1,0:T(8,128)(2,1)} %bitcast.19), calls=%async_computation.2 | async-start | bytes 12582912 | tf_op jit(solution)/shard_map/all_to_all | solution.py:67
  258.8 3.4 collective-permute-start
  262.2 0.1 reduce_sum.21
  262.4 0.0 copy-done.5
  262.4 0.1 copy.34
  262.5 0.0 copy-done.6
  262.5 0.1 copy.35
  262.6 2.0 select_reduce_fusion
  264.7 17.4 %collective-permute-done = f32[2,48,2048]{2,1,0:T(8,128)S(1)} collective-permute-done((f32[2,48,2048]{2,1,0:T(8,128)}, f32[2,48,2048]{2,1,0:T(8,128)S(1)}, u32[]{:S(2)}, u32[]{:S(2)}) %collective-permute-start) | collective-permute-done | bytes 786464 | tf_op jit(solution)/shard_map/ppermute | solution.py:54
  282.0 149.8 %all-to-all-done.2 = bf16[32,2,24,2048]{3,2,1,0:T(8,128)(2,1)} async-done(((bf16[32,2,24,2048]{3,2,1,0:T(8,128)(2,1)}), bf16[32,2,24,2048]{3,2,1,0:T(8,128)(2,1)}, u32[]{:S(2)}, u32[]{:S(2)}) %all-to-all-start.2) | async-done | bytes 6291488 | tf_op jit(solution)/shard_map/all_to_all | solution.py:67
  431.9 3.8 fusion.15
  435.7 4.6 %fusion.4 = bf16[128,2048]{1,0:T(8,128)(2,1)} fusion(f32[128,2048]{1,0:T(8,128)S(1)} %fusion.15, bf16[1536,2048]{1,0:T(8,128)(2,1)} %bitcast.9, f32[128,1536]{1,0:T(8,128)S(1)} %select_reduce_fusion), kind=kOutput, calls=%fused_computation.12 | convolution fusion | flops 806617088 | bytes 8650752 | tf_op jit(solution)/shard_map/dot_general | solution.py:77
  440.3 0.9 copy.42
  (4 shorter events, 0.1 us)
Async XLA Ops:
  0.6 1.6 copy-start
  2.2 20.0 %copy-start.2 = (f32[2,48,2048]{2,1,0:T(8,128)S(1)}, f32[2,48,2048]{2,1,0:T(8,128)}, u32[]{:S(2)}) copy-start(f32[2,48,2048]{2,1,0:T(8,128)} %param.10) | copy-start | bytes 2359300
  2.2 20.0 %copy-start.3 = (bf16[2,48,2048]{2,1,0:T(8,128)(2,1)S(1)}, bf16[2,48,2048]{2,1,0:T(8,128)(2,1)}, u32[]{:S(2)}) copy-start(bf16[2,48,2048]{2,1,0:T(8,128)(2,1)} %param.12) | copy-start | bytes 1179652
  2.2 20.0 %copy-start.4 = (bf16[2,48,2048]{2,1,0:T(8,128)(2,1)S(1)}, bf16[2,48,2048]{2,1,0:T(8,128)(2,1)}, u32[]{:S(2)}) copy-start(bf16[2,48,2048]{2,1,0:T(8,128)(2,1)} %param.13) | copy-start | bytes 1179652
  6.3 76.8 %all-to-all-start = ((bf16[64,24,768]{2,1,0:T(8,128)(2,1)}), bf16[64,24,768]{2,1,0:T(8,128)(2,1)}, u32[]{:S(2)}, u32[]{:S(2)}) async-start(bf16[64,24,768]{2,1,0:T(8,128)(2,1)} %bitcast.22), calls=%async_computation | async-start | bytes 4718592 | tf_op jit(solution)/shard_map/all_to_all | solution.py:63
  86.5 142.4 %all-to-all-start.1 = ((bf16[16,2,48,2048]{3,2,1,0:T(8,128)(2,1)}), bf16[16,2,48,2048]{3,2,1,0:T(8,128)(2,1)}, u32[]{:S(2)}, u32[]{:S(2)}) async-start(bf16[16,2,48,2048]{3,2,1,0:T(8,128)(2,1)} %stack.2), calls=%async_computation.1 | async-start | bytes 12582912 | tf_op jit(solution)/shard_map/all_to_all | solution.py:51
  228.9 3.5 copy-start.1
  240.9 21.5 %copy-start.5 = (s32[128,8]{0,1:T(8,128)S(1)}, s32[128,8]{0,1:T(8,128)}, u32[]{:S(2)}) copy-start(s32[128,8]{0,1:T(8,128)} %param.8) | copy-start | bytes 12292
  240.9 21.7 %copy-start.6 = (s32[128,8]{0,1:T(8,128)S(1)}, s32[128,8]{0,1:T(8,128)}, u32[]{:S(2)}) copy-start(s32[128,8]{0,1:T(8,128)} %param.9) | copy-start | bytes 12292
  240.9 191.0 %all-to-all-start.2 = ((bf16[32,2,24,2048]{3,2,1,0:T(8,128)(2,1)}), bf16[32,2,24,2048]{3,2,1,0:T(8,128)(2,1)}, u32[]{:S(2)}, u32[]{:S(2)}) async-start(bf16[32,2,24,2048]{3,2,1,0:T(8,128)(2,1)} %bitcast.19), calls=%async_computation.2 | async-start | bytes 12582912 | tf_op jit(solution)/shard_map/all_to_all | solution.py:67
  258.8 23.2 %collective-permute-start = (f32[2,48,2048]{2,1,0:T(8,128)}, f32[2,48,2048]{2,1,0:T(8,128)S(1)}, u32[]{:S(2)}, u32[]{:S(2)}) collective-permute-start(f32[2,48,2048]{2,1,0:T(8,128)} %get-tuple-element.3), channel_id=1, source_target_pairs={{0,256},{32,288},{64,320},{96,352},{128,384},{160,416},{192,448},{... | collective-permute-start | bytes 2359304 | tf_op jit(solution)/shard_map/ppermute | solution.py:54
